TPU v7x, 512 devices: a whole 4x4x16 slice. The times are simulated.
512 devices in a mesh: replica: 64 (over z, x), shard: 8 (over y, core).
Axes of the slice: x: 4, y: 4, z: 16, core: 2. Of those that a mesh axis runs over, the one named last changes fastest.
Arguments:
- grad_query: float32 [512, 512, 384], P(('replica', 'shard')), may hold values from -1.25 to 1.25
- grad_output: float32 [512, 384, 512], P(('replica', 'shard')), may hold values from -1.25 to 1.25
- grad_norm: float32 [512, 512], P(('replica', 'shard')), may hold values from -1.25 to 1.25
- grad_bias: float32 [512, 32, 6], P(('replica', 'shard')), may hold values from -0.3 to 0.3
- weight_query: float32 [512, 384], P('shard'), may hold values from -5.303301 to 5.303301
- weight_output: float32 [384, 512], P('shard'), may hold values from -6.1237244 to 6.1237244
- weight_norm: float32 [512], P('shard'), may hold values from 0 to 120
- weight_bias: float32 [32, 6], P('shard'), may hold values from -120 to 120
- first_query: float32 [512, 384], P('shard'), may hold values from -120 to 120
- first_output: float32 [384, 512], P('shard'), may hold values from -120 to 120
- first_norm: float32 [512], P('shard'), may hold values from -120 to 120
- first_bias: float32 [32, 6], P('shard'), may hold values from -120 to 120
- second_query: float32 [512, 384], P('shard'), may hold values from 0.05 to 2
- second_output: float32 [384, 512], P('shard'), may hold values from 0.05 to 2
- second_norm: float32 [512], P('shard'), may hold values from 0.05 to 2
- second_bias: float32 [32, 6], P('shard'), may hold values from 0.05 to 2
Outputs:
- updated_query: bfloat16 [512, 384], replicated
- updated_output: bfloat16 [384, 512], replicated
- updated_norm: bfloat16 [512], replicated
- updated_bias: bfloat16 [32, 6], replicated
- first_query_next: float32 [512, 384], P('shard')
- first_output_next: float32 [384, 512], P('shard')
- first_norm_next: float32 [512], P('shard')
- first_bias_next: float32 [32, 6], P('shard')
- second_query_next: float32 [512, 384], P('shard')
- second_output_next: float32 [384, 512], P('shard')
- second_norm_next: float32 [512], P('shard')
- second_bias_next: float32 [32, 6], P('shard')
- norm_table: float32 [2, 4], replicated
- trust_ratios: float32 [4], replicated
All inputs are finite; a program needn't handle non-finite values.
Results may differ from a plain program's by a relative error of at most 0.008.
Values may be sent and summed in bfloat16 or wider, within the bound.
No kernel may reach another device: no remote copies, remote signals or barrier semaphores. Data moves between devices by JAX's collectives and lax.ppermute only.
A program may use at most 64 MiB of HBM per device.

v0:
```python
import jax
import jax.numpy as jnp
from jax import lax
from jax.sharding import PartitionSpec as P

LANES = 128
SHARD_BITS = (0, 1, 2)
REPLICA_BITS = (3, 5, 4, 6, 7, 8)
AXES = ("replica", "shard")


def step_math(summed, moment, second, weight, decay_rate):
    moment_next = 0.5 * moment + 0.5 * summed
    second_next = 0.5 * second + 0.5 * summed * summed
    update = moment_next / (jnp.sqrt(second_next) + 1e-06) + decay_rate * weight
    return (moment_next, second_next, update)


def padded_width(width, multiple):
    return -(-width // multiple) * multiple


def bit_of(index, bit):
    return index >> bit & 1


def exchange(value, bit, devices):
    return lax.ppermute(value, AXES, [(d, d ^ 1 << bit) for d in range(devices)])


def halve(rows, bits, devices):
    index = lax.axis_index(AXES)
    for bit in bits:
        half = rows.shape[0] // 2
        mine = bit_of(index, bit)
        keep = lax.dynamic_slice_in_dim(rows, mine * half, half, 0)
        send = lax.dynamic_slice_in_dim(rows, (1 - mine) * half, half, 0)
        rows = keep + exchange(send, bit, devices)
    return rows


def double(rows, bits, devices):
    index = lax.axis_index(AXES)
    for bit in reversed(bits):
        other = exchange(rows, bit, devices)
        first = bit_of(index, bit) == 0
        rows = jnp.concatenate(
            [jnp.where(first, rows, other), jnp.where(first, other, rows)], axis=0
        )
    return rows


def on_device(
    grad_query,
    grad_output,
    grad_norm,
    grad_bias,
    weight_query,
    weight_output,
    weight_norm,
    weight_bias,
    first_query,
    first_output,
    first_norm,
    first_bias,
    second_query,
    second_output,
    second_norm,
    second_bias,
    shards,
    replicas,
):
    weights = (weight_query, weight_output, weight_norm, weight_bias)
    moments = (first_query, first_output, first_norm, first_bias)
    seconds = (second_query, second_output, second_norm, second_bias)
    decay_rates = (0.01, 0.01, 0.0, 0.0)
    gradients = (grad_query[0], grad_output[0], grad_norm[0], grad_bias[0])
    sizes = [weight.size for weight in weights]
    offsets = [sum(sizes[:member]) for member in range(4)]
    total = sum(sizes)
    devices = shards * replicas
    width = padded_width(total, LANES * replicas)
    levels = len(SHARD_BITS)
    position = [
        sum(((s >> SHARD_BITS[j] & 1) << levels - 1 - j for j in range(levels)))
        for s in range(shards)
    ]
    blocks = [gradient.reshape(shards, -1) for gradient in gradients]
    filler = jnp.zeros((width - total,), jnp.float32)
    packed = jnp.stack(
        [
            jnp.concatenate([block[position.index(p)] for block in blocks] + [filler])
            for p in range(shards)
        ]
    )
    chunks = packed.reshape(shards * replicas * (width // replicas // LANES), LANES)
    mine = halve(chunks, SHARD_BITS + REPLICA_BITS, devices)
    block = double(mine, REPLICA_BITS, devices)
    summed_flat = block.reshape(width)
    summed_all = [
        summed_flat[offsets[member] : offsets[member] + sizes[member]].reshape(
            weights[member].shape
        )
        for member in range(4)
    ]
    results = [
        step_math(
            summed_all[member],
            moments[member],
            seconds[member],
            weights[member],
            decay_rates[member],
        )
        for member in range(4)
    ]
    weight_squares = [jnp.sum(weight * weight) for weight in weights]
    update_squares = [jnp.sum(result[2] * result[2]) for result in results]
    squares = lax.psum(jnp.stack(weight_squares + update_squares), "shard")
    weight_sizes = jnp.sqrt(squares[:4])
    update_sizes = jnp.sqrt(squares[4:])
    trust_ratios = weight_sizes / (update_sizes + 1e-06)
    shards_out = [
        (weights[member] - 0.01 * trust_ratios[member] * results[member][2])
        .astype(jnp.bfloat16)
        .reshape(-1)
        for member in range(4)
    ]
    out_width = padded_width(total, LANES)
    shards_out.append(jnp.zeros((out_width - total,), jnp.bfloat16))
    gathered = lax.all_gather(jnp.concatenate(shards_out), "shard", axis=0, tiled=False)
    full = [
        gathered[:, offsets[member] : offsets[member] + sizes[member]].reshape(
            (shards * weights[member].shape[0],) + weights[member].shape[1:]
        )
        for member in range(4)
    ]
    norm_table = jnp.stack([weight_sizes, update_sizes])
    return (
        full[0],
        full[1],
        full[2],
        full[3],
        results[0][0],
        results[1][0],
        results[2][0],
        results[3][0],
        results[0][1],
        results[1][1],
        results[2][1],
        results[3][1],
        norm_table,
        trust_ratios,
    )


def solution(mesh):
    shards = mesh.shape["shard"]
    replicas = mesh.shape["replica"]
    placed = (
        P(("replica", "shard"), None, None),
        P(("replica", "shard"), None, None),
        P(("replica", "shard"), None),
        P(("replica", "shard"), None, None),
        P("shard", None),
        P("shard", None),
        P("shard"),
        P("shard", None),
        P("shard", None),
        P("shard", None),
        P("shard"),
        P("shard", None),
        P("shard", None),
        P("shard", None),
        P("shard"),
        P("shard", None),
    )

    def body(*args):
        return on_device(*args, shards=shards, replicas=replicas)

    return jax.shard_map(
        body,
        mesh=mesh,
        in_specs=placed,
        out_specs=(
            P(),
            P(),
            P(),
            P(),
            P("shard", None),
            P("shard", None),
            P("shard"),
            P("shard", None),
            P("shard", None),
            P("shard", None),
            P("shard"),
            P("shard", None),
            P(),
            P(),
        ),
        check_vma=False,
    )
```

profile of v0, /device:TPU:1, one launch (start us, length us, event | category | flops | bytes accessed | tf_op | source)
XLA Modules:
  0.0 204.9 jit_solution(14163425917352322013)
XLA Ops:
  0.7 1.3 slice_bitcast_fusion
  2.2 0.1 fusion.16
  2.3 0.1 copy.59
  2.6 0.1 copy.60
  2.9 0.1 copy.61
  3.1 0.1 copy.62
  4.2 1.0 concatenate.48
  5.1 1.0 concatenate.49
  6.2 1.0 concatenate.50
  7.2 1.0 concatenate.51
  8.2 1.0 concatenate.52
  9.2 1.0 concatenate.45
  10.2 1.0 concatenate.46
  11.2 3.6 %concatenate.47 = f32[57344]{0:T(1024)} concatenate(f32[24576]{0:T(1024)S(1)} %squeeze.108, f32[24576]{0:T(1024)S(1)} %bitcast.90, f32[64]{0:T(128)S(1)} %get-tuple-element.117, f32[24]{0:T(128)S(1)} %squeeze.111, f32[8104]{0:T(1024)S(1)} %broadcast_in_dim.6), dimensions={0} | concatenate | bytes 458752 | tf_op jit(solution)/shard_map/concatenate | solution.py:92
  14.8 4.5 %stack.75 = f32[8,57344]{1,0:T(8,128)S(1)} concatenate(f32[1,57344]{1,0:T(1,128)S(1)} %bitcast.80, f32[1,57344]{1,0:T(1,128)S(1)} %bitcast.81, f32[1,57344]{1,0:T(1,128)} %bitcast.82, f32[1,57344]{1,0:T(1,128)S(1)} %bitcast.75, f32[1,57344]{1,0:T(1,128)S(1)} %bitcast.76, f32[1,57344]{1,0:T(1,128)S(1)} %bitcast.77, f32[1,57344]{1,0:T(1,128)S(1)} %bitcast.78, f32[1,57344]{1,0:T(1,128)S(1)} %bitcast.79), dimensions={0} | concatenate | bytes 3670016 | tf_op jit(solution)/shard_map/stack | solution.py:90
  19.4 1.5 reshape.140
  20.9 1.4 constant_dynamic-slice_fusion.9
  22.3 8.8 %collective-permute-start = (f32[1792,128]{1,0:T(8,128)S(1)}, f32[1792,128]{1,0:T(8,128)}, u32[]{:S(2)}, u32[]{:S(2)}) collective-permute-start(f32[1792,128]{1,0:T(8,128)S(1)} %constant_dynamic-slice_fusion.9), channel_id=1, source_target_pairs={{0,1},{1,0},{2,3},{3,2},{4,5},{5,4},{6,7},{7,6},{8,9},{9,8},{10,11... | collective-permute-start | bytes 2752520 | tf_op jit(solution)/shard_map/ppermute | solution.py:28
  31.1 2.2 %collective-permute-done = f32[1792,128]{1,0:T(8,128)} collective-permute-done((f32[1792,128]{1,0:T(8,128)S(1)}, f32[1792,128]{1,0:T(8,128)}, u32[]{:S(2)}, u32[]{:S(2)}) %collective-permute-start) | collective-permute-done | bytes 917536 | tf_op jit(solution)/shard_map/ppermute | solution.py:28
  33.3 1.3 dynamic-slice_add_fusion
  34.6 1.9 collective-permute-start.1
  36.5 11.7 %collective-permute-done.1 = f32[896,128]{1,0:T(8,128)S(1)} collective-permute-done((f32[896,128]{1,0:T(8,128)S(1)}, f32[896,128]{1,0:T(8,128)S(1)}, u32[]{:S(2)}, u32[]{:S(2)}) %collective-permute-start.1) | collective-permute-done | bytes 458784 | tf_op jit(solution)/shard_map/ppermute | solution.py:28
  48.3 1.9 collective-permute-start.2
  50.3 7.4 %collective-permute-done.2 = f32[448,128]{1,0:T(8,128)S(1)} collective-permute-done((f32[448,128]{1,0:T(8,128)S(1)}, f32[448,128]{1,0:T(8,128)S(1)}, u32[]{:S(2)}, u32[]{:S(2)}) %collective-permute-start.2) | collective-permute-done | bytes 229408 | tf_op jit(solution)/shard_map/ppermute | solution.py:28
  57.7 1.9 collective-permute-start.3
  59.7 3.5 %collective-permute-done.3 = f32[224,128]{1,0:T(8,128)S(1)} collective-permute-done((f32[224,128]{1,0:T(8,128)S(1)}, f32[224,128]{1,0:T(8,128)S(1)}, u32[]{:S(2)}, u32[]{:S(2)}) %collective-permute-start.3) | collective-permute-done | bytes 114720 | tf_op jit(solution)/shard_map/ppermute | solution.py:28
  63.2 1.9 collective-permute-start.4
  65.2 3.0 %collective-permute-done.4 = f32[112,128]{1,0:T(8,128)S(1)} collective-permute-done((f32[112,128]{1,0:T(8,128)S(1)}, f32[112,128]{1,0:T(8,128)S(1)}, u32[]{:S(2)}, u32[]{:S(2)}) %collective-permute-start.4) | collective-permute-done | bytes 57376 | tf_op jit(solution)/shard_map/ppermute | solution.py:28
  68.2 1.9 collective-permute-start.5
  70.2 4.1 %collective-permute-done.5 = f32[56,128]{1,0:T(8,128)S(1)} collective-permute-done((f32[56,128]{1,0:T(8,128)S(1)}, f32[56,128]{1,0:T(8,128)S(1)}, u32[]{:S(2)}, u32[]{:S(2)}) %collective-permute-start.5) | collective-permute-done | bytes 28704 | tf_op jit(solution)/shard_map/ppermute | solution.py:28
  74.3 1.9 collective-permute-start.6
  76.3 3.4 %collective-permute-done.6 = f32[28,128]{1,0:T(8,128)S(1)} collective-permute-done((f32[28,128]{1,0:T(8,128)S(1)}, f32[28,128]{1,0:T(8,128)S(1)}, u32[]{:S(2)}, u32[]{:S(2)}) %collective-permute-start.6) | collective-permute-done | bytes 14368 | tf_op jit(solution)/shard_map/ppermute | solution.py:28
  79.7 4.3 %collective-permute-start.7 = (f32[14,128]{1,0:T(8,128)S(1)}, f32[14,128]{1,0:T(8,128)S(1)}, u32[]{:S(2)}, u32[]{:S(2)}) collective-permute-start(f32[14,128]{1,0:T(8,128)S(1)} %constant_dynamic-slice_fusion.2), channel_id=1, source_target_pairs={{0,128},{1,129},{2,130},{3,131},{4,132},{5,133},{6,134},{7,135},{8... | collective-permute-start | bytes 21512 | tf_op jit(solution)/shard_map/ppermute | solution.py:28
  84.0 4.0 %collective-permute-done.7 = f32[14,128]{1,0:T(8,128)S(1)} collective-permute-done((f32[14,128]{1,0:T(8,128)S(1)}, f32[14,128]{1,0:T(8,128)S(1)}, u32[]{:S(2)}, u32[]{:S(2)}) %collective-permute-start.7) | collective-permute-done | bytes 7200 | tf_op jit(solution)/shard_map/ppermute | solution.py:28
  88.1 10.1 %collective-permute-start.8 = (f32[7,128]{1,0:T(8,128)S(1)}, f32[7,128]{1,0:T(8,128)S(1)}, u32[]{:S(2)}, u32[]{:S(2)}) collective-permute-start(f32[7,128]{1,0:T(8,128)S(1)} %constant_dynamic-slice_fusion), channel_id=1, source_target_pairs={{0,256},{1,257},{2,258},{3,259},{4,260},{5,261},{6,262},{7,263},{8... | collective-permute-start | bytes 10760 | tf_op jit(solution)/shard_map/ppermute | solution.py:28
  98.2 3.0 %collective-permute-done.8 = f32[7,128]{1,0:T(8,128)S(1)} collective-permute-done((f32[7,128]{1,0:T(8,128)S(1)}, f32[7,128]{1,0:T(8,128)S(1)}, u32[]{:S(2)}, u32[]{:S(2)}) %collective-permute-start.8) | collective-permute-done | bytes 3616 | tf_op jit(solution)/shard_map/ppermute | solution.py:28
  101.1 10.1 %collective-permute-start.9 = (f32[7,128]{1,0:T(8,128)S(1)}, f32[7,128]{1,0:T(8,128)S(1)}, u32[]{:S(2)}, u32[]{:S(2)}) collective-permute-start(f32[7,128]{1,0:T(8,128)S(1)} %fusion.5), channel_id=1, source_target_pairs={{0,256},{1,257},{2,258},{3,259},{4,260},{5,261},{6,262},{7,263},{8... | collective-permute-start | bytes 10760 | tf_op jit(solution)/shard_map/ppermute | solution.py:28
  111.2 3.0 %collective-permute-done.9 = f32[7,128]{1,0:T(8,128)S(1)} collective-permute-done((f32[7,128]{1,0:T(8,128)S(1)}, f32[7,128]{1,0:T(8,128)S(1)}, u32[]{:S(2)}, u32[]{:S(2)}) %collective-permute-start.9) | collective-permute-done | bytes 3616 | tf_op jit(solution)/shard_map/ppermute | solution.py:28
  114.2 4.3 %collective-permute-start.10 = (f32[14,128]{1,0:T(8,128)S(1)}, f32[14,128]{1,0:T(8,128)S(1)}, u32[]{:S(2)}, u32[]{:S(2)}) collective-permute-start(f32[14,128]{1,0:T(8,128)S(1)} %pad_maximum_fusion.5), channel_id=1, source_target_pairs={{0,128},{1,129},{2,130},{3,131},{4,132},{5,133},{6,134},{7,135},{8... | collective-permute-start | bytes 21512 | tf_op jit(solution)/shard_map/ppermute | solution.py:28
  118.5 4.3 %collective-permute-done.10 = f32[14,128]{1,0:T(8,128)S(1)} collective-permute-done((f32[14,128]{1,0:T(8,128)S(1)}, f32[14,128]{1,0:T(8,128)S(1)}, u32[]{:S(2)}, u32[]{:S(2)}) %collective-permute-start.10) | collective-permute-done | bytes 7200 | tf_op jit(solution)/shard_map/ppermute | solution.py:28
  122.8 1.9 collective-permute-start.11
  124.8 3.4 %collective-permute-done.11 = f32[28,128]{1,0:T(8,128)S(1)} collective-permute-done((f32[28,128]{1,0:T(8,128)S(1)}, f32[28,128]{1,0:T(8,128)S(1)}, u32[]{:S(2)}, u32[]{:S(2)}) %collective-permute-start.11) | collective-permute-done | bytes 14368 | tf_op jit(solution)/shard_map/ppermute | solution.py:28
  128.2 2.6 %collective-permute-start.12 = (f32[56,128]{1,0:T(8,128)S(1)}, f32[56,128]{1,0:T(8,128)S(1)}, u32[]{:S(2)}, u32[]{:S(2)}) collective-permute-start(f32[56,128]{1,0:T(8,128)S(1)} %pad_maximum_fusion.3), channel_id=1, source_target_pairs={{0,16},{1,17},{2,18},{3,19},{4,20},{5,21},{6,22},{7,23},{8,24},{9,... | collective-permute-start | bytes 86024 | tf_op jit(solution)/shard_map/ppermute | solution.py:28
  130.9 3.5 %collective-permute-done.12 = f32[56,128]{1,0:T(8,128)S(1)} collective-permute-done((f32[56,128]{1,0:T(8,128)S(1)}, f32[56,128]{1,0:T(8,128)S(1)}, u32[]{:S(2)}, u32[]{:S(2)}) %collective-permute-start.12) | collective-permute-done | bytes 28704 | tf_op jit(solution)/shard_map/ppermute | solution.py:28
  134.4 2.0 collective-permute-start.13
  136.4 3.2 %collective-permute-done.13 = f32[112,128]{1,0:T(8,128)S(1)} collective-permute-done((f32[112,128]{1,0:T(8,128)S(1)}, f32[112,128]{1,0:T(8,128)S(1)}, u32[]{:S(2)}, u32[]{:S(2)}) %collective-permute-start.13) | collective-permute-done | bytes 57376 | tf_op jit(solution)/shard_map/ppermute | solution.py:28
  139.6 1.9 collective-permute-start.14
  141.6 3.9 %collective-permute-done.14 = f32[224,128]{1,0:T(8,128)S(1)} collective-permute-done((f32[224,128]{1,0:T(8,128)S(1)}, f32[224,128]{1,0:T(8,128)S(1)}, u32[]{:S(2)}, u32[]{:S(2)}) %collective-permute-start.14) | collective-permute-done | bytes 114720 | tf_op jit(solution)/shard_map/ppermute | solution.py:28
  145.8 1.1 multiply_reduce_fusion.6
  146.9 1.3 multiply_reduce_fusion.4
  148.2 0.7 multiply_reduce_fusion.1
  148.9 0.7 multiply_reduce_fusion
  149.6 5.3 %stack.80 = f32[8]{0:T(128)S(1)} concatenate(f32[1]{0:T(128)} %bitcast, f32[1]{0:T(128)} %bitcast.1, f32[1]{0:T(128)} %bitcast.2, f32[1]{0:T(128)} %bitcast.3, f32[1]{0:T(128)} %bitcast.20, f32[1]{0:T(128)} %bitcast.21, f32[1]{0:T(128)} %bitcast.23, f32[1]{0:T(128)} %bitcast.24), dimensions={0} | concatenate | bytes 64 | tf_op jit(solution)/shard_map/stack | solution.py:118
  154.9 26.8 %psum.7 = f32[8]{0:T(128)S(1)} all-reduce(f32[8]{0:T(128)S(1)} %stack.80), channel_id=1, replica_groups=mesh['replica'=64,'shard'=8] {'shard'}, use_global_device_ids=true, to_apply=%region_8.9 | all-reduce | flops 8 | bytes 64 | tf_op jit(solution)/shard_map/psum | solution.py:118
  181.8 0.6 fusion.17
  185.4 0.1 concatenate.59
  185.5 0.1 reshape.153
  185.6 15.2 %all-gather.1 = bf16[8,1,49280]{2,1,0:T(2,128)(2,1)S(1)} all-gather(bf16[1,1,49280]{2,1,0:T(2,128)(2,1)S(1)} %reshape.153), channel_id=2, replica_groups=mesh['replica'=64,'shard'=8] {'shard'}, dimensions={0}, use_global_device_ids=true | all-gather | bytes 887040 | tf_op jit(solution)/shard_map/all_gather | solution.py:130
  200.8 0.1 copy.76
  201.1 0.9 reshape.148
  202.0 0.9 reshape.149
  203.0 0.7 copy.64
  203.7 0.6 reshape.150
  204.4 0.6 pad_maximum_fusion.6
  (119 shorter events, 2.8 us)
Async XLA Ops:
  0.6 1.5 copy-start.1
  0.7 1.5 copy-start.8
  0.7 1.8 copy-start.14
  20.9 12.4 %copy-start = (f32[3584,128]{1,0:T(8,128)S(1)}, f32[3584,128]{1,0:T(8,128)}, u32[]{:S(2)}) copy-start(f32[3584,128]{1,0:T(8,128)} %reshape.140) | copy-start | bytes 5505028
  22.3 11.0 %collective-permute-start = (f32[1792,128]{1,0:T(8,128)S(1)}, f32[1792,128]{1,0:T(8,128)}, u32[]{:S(2)}, u32[]{:S(2)}) collective-permute-start(f32[1792,128]{1,0:T(8,128)S(1)} %constant_dynamic-slice_fusion.9), channel_id=1, source_target_pairs={{0,1},{1,0},{2,3},{3,2},{4,5},{5,4},{6,7},{7,6},{8,9},{9,8},{10,11... | collective-permute-start | bytes 2752520 | tf_op jit(solution)/shard_map/ppermute | solution.py:28
  34.6 13.6 %collective-permute-start.1 = (f32[896,128]{1,0:T(8,128)S(1)}, f32[896,128]{1,0:T(8,128)S(1)}, u32[]{:S(2)}, u32[]{:S(2)}) collective-permute-start(f32[896,128]{1,0:T(8,128)S(1)} %constant_dynamic-slice_fusion.8), channel_id=1, source_target_pairs={{0,2},{1,3},{2,0},{3,1},{4,6},{5,7},{6,4},{7,5},{8,10},{9,11},{10,... | collective-permute-start | bytes 1376264 | tf_op jit(solution)/shard_map/ppermute | solution.py:28
  48.3 9.3 %collective-permute-start.2 = (f32[448,128]{1,0:T(8,128)S(1)}, f32[448,128]{1,0:T(8,128)S(1)}, u32[]{:S(2)}, u32[]{:S(2)}) collective-permute-start(f32[448,128]{1,0:T(8,128)S(1)} %constant_dynamic-slice_fusion.7), channel_id=1, source_target_pairs={{0,4},{1,5},{2,6},{3,7},{4,0},{5,1},{6,2},{7,3},{8,12},{9,13},{10,... | collective-permute-start | bytes 688136 | tf_op jit(solution)/shard_map/ppermute | solution.py:28
  57.7 5.5 %collective-permute-start.3 = (f32[224,128]{1,0:T(8,128)S(1)}, f32[224,128]{1,0:T(8,128)S(1)}, u32[]{:S(2)}, u32[]{:S(2)}) collective-permute-start(f32[224,128]{1,0:T(8,128)S(1)} %constant_dynamic-slice_fusion.6), channel_id=1, source_target_pairs={{0,8},{1,9},{2,10},{3,11},{4,12},{5,13},{6,14},{7,15},{8,0},{9,1},... | collective-permute-start | bytes 344072 | tf_op jit(solution)/shard_map/ppermute | solution.py:28
  59.6 86.2 %copy-start.18 = (f32[64]{0:T(128)S(1)}, f32[64]{0:T(128)}, u32[]{:S(2)}) copy-start(f32[64]{0:T(128)} %param.22) | copy-start | bytes 772
  59.6 86.2 %copy-start.19 = (f32[64]{0:T(128)S(1)}, f32[64]{0:T(128)}, u32[]{:S(2)}) copy-start(f32[64]{0:T(128)} %param.30) | copy-start | bytes 772
  59.6 86.2 %copy-start.20 = (f32[64]{0:T(128)S(1)}, f32[64]{0:T(128)}, u32[]{:S(2)}) copy-start(f32[64]{0:T(128)} %param.26) | copy-start | bytes 772
  59.6 87.3 %copy-start.15 = (f32[4,6]{1,0:T(4,128)S(1)}, f32[4,6]{1,0:T(4,128)}, u32[]{:S(2)}) copy-start(f32[4,6]{1,0:T(4,128)} %param.23) | copy-start | bytes 292
  59.7 87.3 %copy-start.16 = (f32[4,6]{1,0:T(4,128)S(1)}, f32[4,6]{1,0:T(4,128)}, u32[]{:S(2)}) copy-start(f32[4,6]{1,0:T(4,128)} %param.31) | copy-start | bytes 292
  59.7 87.3 %copy-start.17 = (f32[4,6]{1,0:T(4,128)S(1)}, f32[4,6]{1,0:T(4,128)}, u32[]{:S(2)}) copy-start(f32[4,6]{1,0:T(4,128)} %param.27) | copy-start | bytes 292
  59.7 88.5 %copy-start.3 = (f32[64,384]{1,0:T(8,128)S(1)}, f32[64,384]{1,0:T(8,128)}, u32[]{:S(2)}) copy-start(f32[64,384]{1,0:T(8,128)} %param.20) | copy-start | bytes 294916
  59.7 88.5 %copy-start.9 = (f32[64,384]{1,0:T(8,128)S(1)}, f32[64,384]{1,0:T(8,128)}, u32[]{:S(2)}) copy-start(f32[64,384]{1,0:T(8,128)} %param.28) | copy-start | bytes 294916
  59.7 88.5 %copy-start.10 = (f32[64,384]{1,0:T(8,128)S(1)}, f32[64,384]{1,0:T(8,128)}, u32[]{:S(2)}) copy-start(f32[64,384]{1,0:T(8,128)} %param.24) | copy-start | bytes 294916
  63.2 4.9 %collective-permute-start.4 = (f32[112,128]{1,0:T(8,128)S(1)}, f32[112,128]{1,0:T(8,128)S(1)}, u32[]{:S(2)}, u32[]{:S(2)}) collective-permute-start(f32[112,128]{1,0:T(8,128)S(1)} %constant_dynamic-slice_fusion.5), channel_id=1, source_target_pairs={{0,32},{1,33},{2,34},{3,35},{4,36},{5,37},{6,38},{7,39},{8,40},{9,... | collective-permute-start | bytes 172040 | tf_op jit(solution)/shard_map/ppermute | solution.py:28
  68.2 6.1 %collective-permute-start.5 = (f32[56,128]{1,0:T(8,128)S(1)}, f32[56,128]{1,0:T(8,128)S(1)}, u32[]{:S(2)}, u32[]{:S(2)}) collective-permute-start(f32[56,128]{1,0:T(8,128)S(1)} %constant_dynamic-slice_fusion.4), channel_id=1, source_target_pairs={{0,16},{1,17},{2,18},{3,19},{4,20},{5,21},{6,22},{7,23},{8,24},{9,... | collective-permute-start | bytes 86024 | tf_op jit(solution)/shard_map/ppermute | solution.py:28
  70.1 78.8 %copy-start.2 = (f32[48,512]{1,0:T(8,128)S(1)}, f32[48,512]{1,0:T(8,128)}, u32[]{:S(2)}) copy-start(f32[48,512]{1,0:T(8,128)} %param.21) | copy-start | bytes 294916
  70.1 78.8 %copy-start.11 = (f32[48,512]{1,0:T(8,128)S(1)}, f32[48,512]{1,0:T(8,128)}, u32[]{:S(2)}) copy-start(f32[48,512]{1,0:T(8,128)} %param.29) | copy-start | bytes 294916
  70.2 78.7 %copy-start.12 = (f32[48,512]{1,0:T(8,128)S(1)}, f32[48,512]{1,0:T(8,128)}, u32[]{:S(2)}) copy-start(f32[48,512]{1,0:T(8,128)} %param.25) | copy-start | bytes 294916
  74.3 5.4 %collective-permute-start.6 = (f32[28,128]{1,0:T(8,128)S(1)}, f32[28,128]{1,0:T(8,128)S(1)}, u32[]{:S(2)}, u32[]{:S(2)}) collective-permute-start(f32[28,128]{1,0:T(8,128)S(1)} %constant_dynamic-slice_fusion.3), channel_id=1, source_target_pairs={{0,64},{1,65},{2,66},{3,67},{4,68},{5,69},{6,70},{7,71},{8,72},{9,... | collective-permute-start | bytes 43016 | tf_op jit(solution)/shard_map/ppermute | solution.py:28
  79.7 8.3 %collective-permute-start.7 = (f32[14,128]{1,0:T(8,128)S(1)}, f32[14,128]{1,0:T(8,128)S(1)}, u32[]{:S(2)}, u32[]{:S(2)}) collective-permute-start(f32[14,128]{1,0:T(8,128)S(1)} %constant_dynamic-slice_fusion.2), channel_id=1, source_target_pairs={{0,128},{1,129},{2,130},{3,131},{4,132},{5,133},{6,134},{7,135},{8... | collective-permute-start | bytes 21512 | tf_op jit(solution)/shard_map/ppermute | solution.py:28
  88.1 13.1 %collective-permute-start.8 = (f32[7,128]{1,0:T(8,128)S(1)}, f32[7,128]{1,0:T(8,128)S(1)}, u32[]{:S(2)}, u32[]{:S(2)}) collective-permute-start(f32[7,128]{1,0:T(8,128)S(1)} %constant_dynamic-slice_fusion), channel_id=1, source_target_pairs={{0,256},{1,257},{2,258},{3,259},{4,260},{5,261},{6,262},{7,263},{8... | collective-permute-start | bytes 10760 | tf_op jit(solution)/shard_map/ppermute | solution.py:28
  101.1 13.1 %collective-permute-start.9 = (f32[7,128]{1,0:T(8,128)S(1)}, f32[7,128]{1,0:T(8,128)S(1)}, u32[]{:S(2)}, u32[]{:S(2)}) collective-permute-start(f32[7,128]{1,0:T(8,128)S(1)} %fusion.5), channel_id=1, source_target_pairs={{0,256},{1,257},{2,258},{3,259},{4,260},{5,261},{6,262},{7,263},{8... | collective-permute-start | bytes 10760 | tf_op jit(solution)/shard_map/ppermute | solution.py:28
  114.2 8.6 %collective-permute-start.10 = (f32[14,128]{1,0:T(8,128)S(1)}, f32[14,128]{1,0:T(8,128)S(1)}, u32[]{:S(2)}, u32[]{:S(2)}) collective-permute-start(f32[14,128]{1,0:T(8,128)S(1)} %pad_maximum_fusion.5), channel_id=1, source_target_pairs={{0,128},{1,129},{2,130},{3,131},{4,132},{5,133},{6,134},{7,135},{8... | collective-permute-start | bytes 21512 | tf_op jit(solution)/shard_map/ppermute | solution.py:28
  122.8 5.4 %collective-permute-start.11 = (f32[28,128]{1,0:T(8,128)S(1)}, f32[28,128]{1,0:T(8,128)S(1)}, u32[]{:S(2)}, u32[]{:S(2)}) collective-permute-start(f32[28,128]{1,0:T(8,128)S(1)} %pad_maximum_fusion.4), channel_id=1, source_target_pairs={{0,64},{1,65},{2,66},{3,67},{4,68},{5,69},{6,70},{7,71},{8,72},{9,... | collective-permute-start | bytes 43016 | tf_op jit(solution)/shard_map/ppermute | solution.py:28
  128.2 6.1 %collective-permute-start.12 = (f32[56,128]{1,0:T(8,128)S(1)}, f32[56,128]{1,0:T(8,128)S(1)}, u32[]{:S(2)}, u32[]{:S(2)}) collective-permute-start(f32[56,128]{1,0:T(8,128)S(1)} %pad_maximum_fusion.3), channel_id=1, source_target_pairs={{0,16},{1,17},{2,18},{3,19},{4,20},{5,21},{6,22},{7,23},{8,24},{9,... | collective-permute-start | bytes 86024 | tf_op jit(solution)/shard_map/ppermute | solution.py:28
  134.4 5.2 %collective-permute-start.13 = (f32[112,128]{1,0:T(8,128)S(1)}, f32[112,128]{1,0:T(8,128)S(1)}, u32[]{:S(2)}, u32[]{:S(2)}) collective-permute-start(f32[112,128]{1,0:T(8,128)S(1)} %pad_maximum_fusion.2), channel_id=1, source_target_pairs={{0,32},{1,33},{2,34},{3,35},{4,36},{5,37},{6,38},{7,39},{8,40},{9,... | collective-permute-start | bytes 172040 | tf_op jit(solution)/shard_map/ppermute | solution.py:28
  139.6 5.8 %collective-permute-start.14 = (f32[224,128]{1,0:T(8,128)S(1)}, f32[224,128]{1,0:T(8,128)S(1)}, u32[]{:S(2)}, u32[]{:S(2)}) collective-permute-start(f32[224,128]{1,0:T(8,128)S(1)} %pad_maximum_fusion.1), channel_id=1, source_target_pairs={{0,8},{1,9},{2,10},{3,11},{4,12},{5,13},{6,14},{7,15},{8,0},{9,1},... | collective-permute-start | bytes 344072 | tf_op jit(solution)/shard_map/ppermute | solution.py:28
  148.9 51.9 %copy-start.4 = (f32[64,384]{1,0:T(8,128)}, f32[64,384]{1,0:T(8,128)S(1)}, u32[]{:S(2)}) copy-start(f32[64,384]{1,0:T(8,128)S(1)} %get-tuple-element.70) | copy-start | bytes 294916
  148.9 51.9 %copy-start.5 = (f32[64,384]{1,0:T(8,128)}, f32[64,384]{1,0:T(8,128)S(1)}, u32[]{:S(2)}) copy-start(f32[64,384]{1,0:T(8,128)S(1)} %get-tuple-element.71) | copy-start | bytes 294916
  149.6 51.3 %copy-start.6 = (f32[48,512]{1,0:T(8,128)}, f32[48,512]{1,0:T(8,128)S(1)}, u32[]{:S(2)}) copy-start(f32[48,512]{1,0:T(8,128)S(1)} %get-tuple-element.68) | copy-start | bytes 294916
  149.6 51.3 %copy-start.7 = (f32[48,512]{1,0:T(8,128)}, f32[48,512]{1,0:T(8,128)S(1)}, u32[]{:S(2)}) copy-start(f32[48,512]{1,0:T(8,128)S(1)} %get-tuple-element.69) | copy-start | bytes 294916
  181.8 19.1 %copy-start.13 = (f32[4]{0:T(128)}, f32[4]{0:T(128)S(1)}, u32[]{:S(2)}) copy-start(f32[4]{0:T(128)S(1)} %get-tuple-element.123) | copy-start | bytes 52
where the time goes:
time: 206 us; the launch traced here: 205 us
  waiting for transfers between devices  63.6 us (31%)
  starting transfers between devices  57.5 us (28%)
  blocking collectives  42 us (20%)
  local copies, waits for them, and re-layouts  31.6 us (15%)
  other arithmetic  6.09 us (3%)
  between operations  4.1 us (2%)
    ppermute x15, waiting for transfers between devices, exchange(): lax.ppermute(value, AXES, [(d, d ^ 1 << bit) for d in range(devices)])  63.6 us
    ppermute x15, starting transfers between devices, exchange(): lax.ppermute(value, AXES, [(d, d ^ 1 << bit) for d in range(devices)])  57.5 us
    psum x1, blocking collectives, on_device(): squares = lax.psum(jnp.stack(weight_squares + update_squares), 'shard')  26.8 us
    all_gather x1, blocking collectives, on_device(): lax.all_gather(jnp.concatenate(shards_out), 'shard', axis=0, tiled=False)  15.2 us
    concatenate x8, local copies, waits for them, and re-layouts, on_device(): jnp.concatenate([block[position.index(p)] for block in blocks] + [filler])  10.6 us
    another operation x1, local copies, waits for them, and re-layouts, on_device(): squares = lax.psum(jnp.stack(weight_squares + update_squares), 'shard')  5.32 us
    another operation x1, local copies, waits for them, and re-layouts, on_device(): jnp.stack([jnp.concatenate([block[position.index(p)] for block in blocks]...  4.55 us
  transfers between devices with their start and end apart: 15, of which 15 were waited for; matrix products, arithmetic and copies ran while one was open for 0% of the time, Pallas kernels for 0%

commit v1 on v0

--- a/solution.py
+++ b/solution.py
@@ -115,7 +115,8 @@
     ]
     weight_squares = [jnp.sum(weight * weight) for weight in weights]
     update_squares = [jnp.sum(result[2] * result[2]) for result in results]
-    squares = lax.psum(jnp.stack(weight_squares + update_squares), "shard")
+    xin = jnp.stack(weight_squares + update_squares)
+    squares = jnp.sum(lax.all_gather(xin, axis_name="shard"), axis=0)
     weight_sizes = jnp.sqrt(squares[:4])
     update_sizes = jnp.sqrt(squares[4:])
     trust_ratios = weight_sizes / (update_sizes + 1e-06)

time: 206 us -> 206 us (level)
    psum x1 -> x0, blocking collectives: 26.8 us -> none  [on_device(): squares = lax.psum(jnp.stack(weight_squares + update_squares), 'shard')]
    unnamed x0 -> x1, blocking collectives: none -> 26.8 us
  transfers between devices with their start and end apart: 15 -> 15, of which waited for: 15 -> 15; matrix products, arithmetic and copies ran while one was open for 0% -> 1% of each run, Pallas kernels for 0% -> 0%
where the time goes in v1:
time: 206 us; the launch traced here: 205 us
  waiting for transfers between devices  61.7 us (30%)
  starting transfers between devices  57.6 us (28%)
  blocking collectives  42 us (20%)
  local copies, waits for them, and re-layouts  33.1 us (16%)
  other arithmetic  6.11 us (3%)
  between operations  4.76 us (2%)
    ppermute x15, waiting for transfers between devices, exchange(): lax.ppermute(value, AXES, [(d, d ^ 1 << bit) for d in range(devices)])  61.7 us
    ppermute x15, starting transfers between devices, exchange(): lax.ppermute(value, AXES, [(d, d ^ 1 << bit) for d in range(devices)])  57.6 us
    unnamed x1, blocking collectives  26.8 us
    all_gather x1, blocking collectives, on_device(): lax.all_gather(jnp.concatenate(shards_out), 'shard', axis=0, tiled=False)  15.2 us
    concatenate x8, local copies, waits for them, and re-layouts, on_device(): jnp.concatenate([block[position.index(p)] for block in blocks] + [filler])  10.6 us
    another operation x1, local copies, waits for them, and re-layouts, on_device(): xin = jnp.stack(weight_squares + update_squares)  5.22 us
    another operation x1, local copies, waits for them, and re-layouts, on_device(): jnp.stack([jnp.concatenate([block[position.index(p)] for block in blocks]...  4.55 us
  transfers between devices with their start and end apart: 15, of which 15 were waited for; matrix products, arithmetic and copies ran while one was open for 1% of the time, Pallas kernels for 0%

profile of v1, /device:TPU:1, one launch (start us, length us, event | category | flops | bytes accessed | tf_op | source)
XLA Modules:
  0.0 205.3 jit_solution(4084951005706063503)
XLA Ops:
  0.7 1.3 slice_bitcast_fusion
  2.2 0.1 fusion.16
  2.6 0.1 copy.60
  2.9 0.1 copy.61
  4.2 1.0 concatenate.48
  5.1 1.0 concatenate.49
  6.2 1.0 concatenate.50
  7.2 1.0 concatenate.51
  8.2 1.0 concatenate.52
  9.2 1.0 concatenate.45
  10.2 1.0 concatenate.46
  11.2 3.6 %concatenate.47 = f32[57344]{0:T(1024)} concatenate(f32[24576]{0:T(1024)S(1)} %squeeze.108, f32[24576]{0:T(1024)S(1)} %bitcast.91, f32[64]{0:T(128)S(1)} %get-tuple-element.117, f32[24]{0:T(128)S(1)} %squeeze.111, f32[8104]{0:T(1024)S(1)} %broadcast_in_dim.6), dimensions={0} | concatenate | bytes 458752 | tf_op jit(solution)/shard_map/concatenate | solution.py:92
  14.8 4.5 %stack.75 = f32[8,57344]{1,0:T(8,128)S(1)} concatenate(f32[1,57344]{1,0:T(1,128)S(1)} %bitcast.81, f32[1,57344]{1,0:T(1,128)S(1)} %bitcast.82, f32[1,57344]{1,0:T(1,128)} %bitcast.83, f32[1,57344]{1,0:T(1,128)S(1)} %bitcast.76, f32[1,57344]{1,0:T(1,128)S(1)} %bitcast.77, f32[1,57344]{1,0:T(1,128)S(1)} %bitcast.78, f32[1,57344]{1,0:T(1,128)S(1)} %bitcast.79, f32[1,57344]{1,0:T(1,128)S(1)} %bitcast.80), dimensions={0} | concatenate | bytes 3670016 | tf_op jit(solution)/shard_map/stack | solution.py:90
  19.4 1.5 reshape.140
  20.9 1.4 constant_dynamic-slice_fusion.9
  22.3 8.8 %collective-permute-start = (f32[1792,128]{1,0:T(8,128)S(1)}, f32[1792,128]{1,0:T(8,128)}, u32[]{:S(2)}, u32[]{:S(2)}) collective-permute-start(f32[1792,128]{1,0:T(8,128)S(1)} %constant_dynamic-slice_fusion.9), channel_id=1, source_target_pairs={{0,1},{1,0},{2,3},{3,2},{4,5},{5,4},{6,7},{7,6},{8,9},{9,8},{10,11... | collective-permute-start | bytes 2752520 | tf_op jit(solution)/shard_map/ppermute | solution.py:28
  31.1 2.2 %collective-permute-done = f32[1792,128]{1,0:T(8,128)} collective-permute-done((f32[1792,128]{1,0:T(8,128)S(1)}, f32[1792,128]{1,0:T(8,128)}, u32[]{:S(2)}, u32[]{:S(2)}) %collective-permute-start) | collective-permute-done | bytes 917536 | tf_op jit(solution)/shard_map/ppermute | solution.py:28
  33.3 1.3 dynamic-slice_add_fusion
  34.6 1.9 collective-permute-start.1
  36.6 11.7 %collective-permute-done.1 = f32[896,128]{1,0:T(8,128)S(1)} collective-permute-done((f32[896,128]{1,0:T(8,128)S(1)}, f32[896,128]{1,0:T(8,128)S(1)}, u32[]{:S(2)}, u32[]{:S(2)}) %collective-permute-start.1) | collective-permute-done | bytes 458784 | tf_op jit(solution)/shard_map/ppermute | solution.py:28
  48.3 1.9 collective-permute-start.2
  50.3 7.4 %collective-permute-done.2 = f32[448,128]{1,0:T(8,128)S(1)} collective-permute-done((f32[448,128]{1,0:T(8,128)S(1)}, f32[448,128]{1,0:T(8,128)S(1)}, u32[]{:S(2)}, u32[]{:S(2)}) %collective-permute-start.2) | collective-permute-done | bytes 229408 | tf_op jit(solution)/shard_map/ppermute | solution.py:28
  57.7 1.9 collective-permute-start.3
  59.7 3.5 %collective-permute-done.3 = f32[224,128]{1,0:T(8,128)S(1)} collective-permute-done((f32[224,128]{1,0:T(8,128)S(1)}, f32[224,128]{1,0:T(8,128)S(1)}, u32[]{:S(2)}, u32[]{:S(2)}) %collective-permute-start.3) | collective-permute-done | bytes 114720 | tf_op jit(solution)/shard_map/ppermute | solution.py:28
  63.3 2.1 collective-permute-start.4
  65.4 3.0 %collective-permute-done.4 = f32[112,128]{1,0:T(8,128)S(1)} collective-permute-done((f32[112,128]{1,0:T(8,128)S(1)}, f32[112,128]{1,0:T(8,128)S(1)}, u32[]{:S(2)}, u32[]{:S(2)}) %collective-permute-start.4) | collective-permute-done | bytes 57376 | tf_op jit(solution)/shard_map/ppermute | solution.py:28
  68.4 1.9 collective-permute-start.5
  70.4 4.1 %collective-permute-done.5 = f32[56,128]{1,0:T(8,128)S(1)} collective-permute-done((f32[56,128]{1,0:T(8,128)S(1)}, f32[56,128]{1,0:T(8,128)S(1)}, u32[]{:S(2)}, u32[]{:S(2)}) %collective-permute-start.5) | collective-permute-done | bytes 28704 | tf_op jit(solution)/shard_map/ppermute | solution.py:28
  74.5 1.9 collective-permute-start.6
  76.5 3.4 %collective-permute-done.6 = f32[28,128]{1,0:T(8,128)S(1)} collective-permute-done((f32[28,128]{1,0:T(8,128)S(1)}, f32[28,128]{1,0:T(8,128)S(1)}, u32[]{:S(2)}, u32[]{:S(2)}) %collective-permute-start.6) | collective-permute-done | bytes 14368 | tf_op jit(solution)/shard_map/ppermute | solution.py:28
  79.9 4.3 %collective-permute-start.7 = (f32[14,128]{1,0:T(8,128)S(1)}, f32[14,128]{1,0:T(8,128)S(1)}, u32[]{:S(2)}, u32[]{:S(2)}) collective-permute-start(f32[14,128]{1,0:T(8,128)S(1)} %constant_dynamic-slice_fusion.2), channel_id=1, source_target_pairs={{0,128},{1,129},{2,130},{3,131},{4,132},{5,133},{6,134},{7,135},{8... | collective-permute-start | bytes 21512 | tf_op jit(solution)/shard_map/ppermute | solution.py:28
  84.2 4.0 %collective-permute-done.7 = f32[14,128]{1,0:T(8,128)S(1)} collective-permute-done((f32[14,128]{1,0:T(8,128)S(1)}, f32[14,128]{1,0:T(8,128)S(1)}, u32[]{:S(2)}, u32[]{:S(2)}) %collective-permute-start.7) | collective-permute-done | bytes 7200 | tf_op jit(solution)/shard_map/ppermute | solution.py:28
  88.3 10.1 %collective-permute-start.8 = (f32[7,128]{1,0:T(8,128)S(1)}, f32[7,128]{1,0:T(8,128)S(1)}, u32[]{:S(2)}, u32[]{:S(2)}) collective-permute-start(f32[7,128]{1,0:T(8,128)S(1)} %constant_dynamic-slice_fusion), channel_id=1, source_target_pairs={{0,256},{1,257},{2,258},{3,259},{4,260},{5,261},{6,262},{7,263},{8... | collective-permute-start | bytes 10760 | tf_op jit(solution)/shard_map/ppermute | solution.py:28
  98.3 3.0 %collective-permute-done.8 = f32[7,128]{1,0:T(8,128)S(1)} collective-permute-done((f32[7,128]{1,0:T(8,128)S(1)}, f32[7,128]{1,0:T(8,128)S(1)}, u32[]{:S(2)}, u32[]{:S(2)}) %collective-permute-start.8) | collective-permute-done | bytes 3616 | tf_op jit(solution)/shard_map/ppermute | solution.py:28
  101.3 10.1 %collective-permute-start.9 = (f32[7,128]{1,0:T(8,128)S(1)}, f32[7,128]{1,0:T(8,128)S(1)}, u32[]{:S(2)}, u32[]{:S(2)}) collective-permute-start(f32[7,128]{1,0:T(8,128)S(1)} %fusion.5), channel_id=1, source_target_pairs={{0,256},{1,257},{2,258},{3,259},{4,260},{5,261},{6,262},{7,263},{8... | collective-permute-start | bytes 10760 | tf_op jit(solution)/shard_map/ppermute | solution.py:28
  111.4 3.0 %collective-permute-done.9 = f32[7,128]{1,0:T(8,128)S(1)} collective-permute-done((f32[7,128]{1,0:T(8,128)S(1)}, f32[7,128]{1,0:T(8,128)S(1)}, u32[]{:S(2)}, u32[]{:S(2)}) %collective-permute-start.9) | collective-permute-done | bytes 3616 | tf_op jit(solution)/shard_map/ppermute | solution.py:28
  114.4 4.3 %collective-permute-start.10 = (f32[14,128]{1,0:T(8,128)S(1)}, f32[14,128]{1,0:T(8,128)S(1)}, u32[]{:S(2)}, u32[]{:S(2)}) collective-permute-start(f32[14,128]{1,0:T(8,128)S(1)} %pad_maximum_fusion.5), channel_id=1, source_target_pairs={{0,128},{1,129},{2,130},{3,131},{4,132},{5,133},{6,134},{7,135},{8... | collective-permute-start | bytes 21512 | tf_op jit(solution)/shard_map/ppermute | solution.py:28
  118.7 4.3 %collective-permute-done.10 = f32[14,128]{1,0:T(8,128)S(1)} collective-permute-done((f32[14,128]{1,0:T(8,128)S(1)}, f32[14,128]{1,0:T(8,128)S(1)}, u32[]{:S(2)}, u32[]{:S(2)}) %collective-permute-start.10) | collective-permute-done | bytes 7200 | tf_op jit(solution)/shard_map/ppermute | solution.py:28
  123.0 1.9 collective-permute-start.11
  125.0 3.4 %collective-permute-done.11 = f32[28,128]{1,0:T(8,128)S(1)} collective-permute-done((f32[28,128]{1,0:T(8,128)S(1)}, f32[28,128]{1,0:T(8,128)S(1)}, u32[]{:S(2)}, u32[]{:S(2)}) %collective-permute-start.11) | collective-permute-done | bytes 14368 | tf_op jit(solution)/shard_map/ppermute | solution.py:28
  128.4 2.6 %collective-permute-start.12 = (f32[56,128]{1,0:T(8,128)S(1)}, f32[56,128]{1,0:T(8,128)S(1)}, u32[]{:S(2)}, u32[]{:S(2)}) collective-permute-start(f32[56,128]{1,0:T(8,128)S(1)} %pad_maximum_fusion.3), channel_id=1, source_target_pairs={{0,16},{1,17},{2,18},{3,19},{4,20},{5,21},{6,22},{7,23},{8,24},{9,... | collective-permute-start | bytes 86024 | tf_op jit(solution)/shard_map/ppermute | solution.py:28
  131.1 3.5 %collective-permute-done.12 = f32[56,128]{1,0:T(8,128)S(1)} collective-permute-done((f32[56,128]{1,0:T(8,128)S(1)}, f32[56,128]{1,0:T(8,128)S(1)}, u32[]{:S(2)}, u32[]{:S(2)}) %collective-permute-start.12) | collective-permute-done | bytes 28704 | tf_op jit(solution)/shard_map/ppermute | solution.py:28
  134.6 2.0 collective-permute-start.13
  136.6 3.2 %collective-permute-done.13 = f32[112,128]{1,0:T(8,128)S(1)} collective-permute-done((f32[112,128]{1,0:T(8,128)S(1)}, f32[112,128]{1,0:T(8,128)S(1)}, u32[]{:S(2)}, u32[]{:S(2)}) %collective-permute-start.13) | collective-permute-done | bytes 57376 | tf_op jit(solution)/shard_map/ppermute | solution.py:28
  139.8 1.9 collective-permute-start.14
  141.8 1.3 dynamic-slice
  143.7 2.0 collective-permute-done.14
  146.0 1.1 multiply_reduce_fusion.6
  147.1 1.3 multiply_reduce_fusion.4
  148.4 0.7 multiply_reduce_fusion.1
  149.1 0.7 multiply_reduce_fusion
  149.8 5.2 %stack.80 = f32[8]{0:T(128)S(1)} concatenate(f32[1]{0:T(128)} %bitcast, f32[1]{0:T(128)} %bitcast.1, f32[1]{0:T(128)} %bitcast.2, f32[1]{0:T(128)} %bitcast.3, f32[1]{0:T(128)} %bitcast.20, f32[1]{0:T(128)} %bitcast.21, f32[1]{0:T(128)} %bitcast.23, f32[1]{0:T(128)} %bitcast.24), dimensions={0} | concatenate | bytes 64 | tf_op jit(solution)/shard_map/stack | solution.py:118
  155.0 0.2 dynamic-update-slice
  155.2 26.8 %all-reduce = f32[64]{0:T(128)S(1)} all-reduce(f32[64]{0:T(128)S(1)} %dynamic-update-slice), channel_id=2, replica_groups=mesh['replica'=64,'shard'=8] {'shard'}, use_global_device_ids=true, to_apply=%add | all-reduce | flops 64 | bytes 512
  182.2 0.6 fusion.17
  185.8 0.1 concatenate.59
  185.9 0.1 reshape.157
  186.0 15.2 %all-gather.2 = bf16[8,1,49280]{2,1,0:T(2,128)(2,1)S(1)} all-gather(bf16[1,1,49280]{2,1,0:T(2,128)(2,1)S(1)} %reshape.157), channel_id=3, replica_groups=mesh['replica'=64,'shard'=8] {'shard'}, dimensions={0}, use_global_device_ids=true | all-gather | bytes 887040 | tf_op jit(solution)/shard_map/all_gather | solution.py:131
  201.2 0.1 copy.76
  201.5 0.9 reshape.148
  202.4 0.9 reshape.149
  203.4 0.7 copy.64
  204.1 0.6 reshape.150
  204.8 0.6 pad_maximum_fusion.6
  (124 shorter events, 3.1 us)
Async XLA Ops:
  0.6 1.5 copy-start.1
  0.7 1.5 copy-start.8
  0.7 1.8 copy-start.14
  20.9 12.4 %copy-start = (f32[3584,128]{1,0:T(8,128)S(1)}, f32[3584,128]{1,0:T(8,128)}, u32[]{:S(2)}) copy-start(f32[3584,128]{1,0:T(8,128)} %reshape.140) | copy-start | bytes 5505028
  22.3 11.0 %collective-permute-start = (f32[1792,128]{1,0:T(8,128)S(1)}, f32[1792,128]{1,0:T(8,128)}, u32[]{:S(2)}, u32[]{:S(2)}) collective-permute-start(f32[1792,128]{1,0:T(8,128)S(1)} %constant_dynamic-slice_fusion.9), channel_id=1, source_target_pairs={{0,1},{1,0},{2,3},{3,2},{4,5},{5,4},{6,7},{7,6},{8,9},{9,8},{10,11... | collective-permute-start | bytes 2752520 | tf_op jit(solution)/shard_map/ppermute | solution.py:28
  34.6 13.6 %collective-permute-start.1 = (f32[896,128]{1,0:T(8,128)S(1)}, f32[896,128]{1,0:T(8,128)S(1)}, u32[]{:S(2)}, u32[]{:S(2)}) collective-permute-start(f32[896,128]{1,0:T(8,128)S(1)} %constant_dynamic-slice_fusion.8), channel_id=1, source_target_pairs={{0,2},{1,3},{2,0},{3,1},{4,6},{5,7},{6,4},{7,5},{8,10},{9,11},{10,... | collective-permute-start | bytes 1376264 | tf_op jit(solution)/shard_map/ppermute | solution.py:28
  48.3 9.3 %collective-permute-start.2 = (f32[448,128]{1,0:T(8,128)S(1)}, f32[448,128]{1,0:T(8,128)S(1)}, u32[]{:S(2)}, u32[]{:S(2)}) collective-permute-start(f32[448,128]{1,0:T(8,128)S(1)} %constant_dynamic-slice_fusion.7), channel_id=1, source_target_pairs={{0,4},{1,5},{2,6},{3,7},{4,0},{5,1},{6,2},{7,3},{8,12},{9,13},{10,... | collective-permute-start | bytes 688136 | tf_op jit(solution)/shard_map/ppermute | solution.py:28
  57.7 5.5 %collective-permute-start.3 = (f32[224,128]{1,0:T(8,128)S(1)}, f32[224,128]{1,0:T(8,128)S(1)}, u32[]{:S(2)}, u32[]{:S(2)}) collective-permute-start(f32[224,128]{1,0:T(8,128)S(1)} %constant_dynamic-slice_fusion.6), channel_id=1, source_target_pairs={{0,8},{1,9},{2,10},{3,11},{4,12},{5,13},{6,14},{7,15},{8,0},{9,1},... | collective-permute-start | bytes 344072 | tf_op jit(solution)/shard_map/ppermute | solution.py:28
  59.6 86.3 %copy-start.18 = (f32[64]{0:T(128)S(1)}, f32[64]{0:T(128)}, u32[]{:S(2)}) copy-start(f32[64]{0:T(128)} %param.22) | copy-start | bytes 772
  59.6 86.3 %copy-start.19 = (f32[64]{0:T(128)S(1)}, f32[64]{0:T(128)}, u32[]{:S(2)}) copy-start(f32[64]{0:T(128)} %param.30) | copy-start | bytes 772
  59.6 86.3 %copy-start.20 = (f32[64]{0:T(128)S(1)}, f32[64]{0:T(128)}, u32[]{:S(2)}) copy-start(f32[64]{0:T(128)} %param.26) | copy-start | bytes 772
  59.7 87.5 %copy-start.15 = (f32[4,6]{1,0:T(4,128)S(1)}, f32[4,6]{1,0:T(4,128)}, u32[]{:S(2)}) copy-start(f32[4,6]{1,0:T(4,128)} %param.23) | copy-start | bytes 292
  59.7 87.4 %copy-start.16 = (f32[4,6]{1,0:T(4,128)S(1)}, f32[4,6]{1,0:T(4,128)}, u32[]{:S(2)}) copy-start(f32[4,6]{1,0:T(4,128)} %param.31) | copy-start | bytes 292
  59.7 87.4 %copy-start.17 = (f32[4,6]{1,0:T(4,128)S(1)}, f32[4,6]{1,0:T(4,128)}, u32[]{:S(2)}) copy-start(f32[4,6]{1,0:T(4,128)} %param.27) | copy-start | bytes 292
  63.2 85.2 %copy-start.3 = (f32[64,384]{1,0:T(8,128)S(1)}, f32[64,384]{1,0:T(8,128)}, u32[]{:S(2)}) copy-start(f32[64,384]{1,0:T(8,128)} %param.20) | copy-start | bytes 294916
  63.2 85.1 %copy-start.9 = (f32[64,384]{1,0:T(8,128)S(1)}, f32[64,384]{1,0:T(8,128)}, u32[]{:S(2)}) copy-start(f32[64,384]{1,0:T(8,128)} %param.28) | copy-start | bytes 294916
  63.3 85.1 %copy-start.10 = (f32[64,384]{1,0:T(8,128)S(1)}, f32[64,384]{1,0:T(8,128)}, u32[]{:S(2)}) copy-start(f32[64,384]{1,0:T(8,128)} %param.24) | copy-start | bytes 294916
  63.3 5.1 %collective-permute-start.4 = (f32[112,128]{1,0:T(8,128)S(1)}, f32[112,128]{1,0:T(8,128)S(1)}, u32[]{:S(2)}, u32[]{:S(2)}) collective-permute-start(f32[112,128]{1,0:T(8,128)S(1)} %constant_dynamic-slice_fusion.5), channel_id=1, source_target_pairs={{0,32},{1,33},{2,34},{3,35},{4,36},{5,37},{6,38},{7,39},{8,40},{9,... | collective-permute-start | bytes 172040 | tf_op jit(solution)/shard_map/ppermute | solution.py:28
  68.4 6.1 %collective-permute-start.5 = (f32[56,128]{1,0:T(8,128)S(1)}, f32[56,128]{1,0:T(8,128)S(1)}, u32[]{:S(2)}, u32[]{:S(2)}) collective-permute-start(f32[56,128]{1,0:T(8,128)S(1)} %constant_dynamic-slice_fusion.4), channel_id=1, source_target_pairs={{0,16},{1,17},{2,18},{3,19},{4,20},{5,21},{6,22},{7,23},{8,24},{9,... | collective-permute-start | bytes 86024 | tf_op jit(solution)/shard_map/ppermute | solution.py:28
  70.3 78.8 %copy-start.2 = (f32[48,512]{1,0:T(8,128)S(1)}, f32[48,512]{1,0:T(8,128)}, u32[]{:S(2)}) copy-start(f32[48,512]{1,0:T(8,128)} %param.21) | copy-start | bytes 294916
  70.3 78.8 %copy-start.11 = (f32[48,512]{1,0:T(8,128)S(1)}, f32[48,512]{1,0:T(8,128)}, u32[]{:S(2)}) copy-start(f32[48,512]{1,0:T(8,128)} %param.29) | copy-start | bytes 294916
  70.3 78.7 %copy-start.12 = (f32[48,512]{1,0:T(8,128)S(1)}, f32[48,512]{1,0:T(8,128)}, u32[]{:S(2)}) copy-start(f32[48,512]{1,0:T(8,128)} %param.25) | copy-start | bytes 294916
  74.5 5.4 %collective-permute-start.6 = (f32[28,128]{1,0:T(8,128)S(1)}, f32[28,128]{1,0:T(8,128)S(1)}, u32[]{:S(2)}, u32[]{:S(2)}) collective-permute-start(f32[28,128]{1,0:T(8,128)S(1)} %constant_dynamic-slice_fusion.3), channel_id=1, source_target_pairs={{0,64},{1,65},{2,66},{3,67},{4,68},{5,69},{6,70},{7,71},{8,72},{9,... | collective-permute-start | bytes 43016 | tf_op jit(solution)/shard_map/ppermute | solution.py:28
  79.9 8.3 %collective-permute-start.7 = (f32[14,128]{1,0:T(8,128)S(1)}, f32[14,128]{1,0:T(8,128)S(1)}, u32[]{:S(2)}, u32[]{:S(2)}) collective-permute-start(f32[14,128]{1,0:T(8,128)S(1)} %constant_dynamic-slice_fusion.2), channel_id=1, source_target_pairs={{0,128},{1,129},{2,130},{3,131},{4,132},{5,133},{6,134},{7,135},{8... | collective-permute-start | bytes 21512 | tf_op jit(solution)/shard_map/ppermute | solution.py:28
  88.3 13.1 %collective-permute-start.8 = (f32[7,128]{1,0:T(8,128)S(1)}, f32[7,128]{1,0:T(8,128)S(1)}, u32[]{:S(2)}, u32[]{:S(2)}) collective-permute-start(f32[7,128]{1,0:T(8,128)S(1)} %constant_dynamic-slice_fusion), channel_id=1, source_target_pairs={{0,256},{1,257},{2,258},{3,259},{4,260},{5,261},{6,262},{7,263},{8... | collective-permute-start | bytes 10760 | tf_op jit(solution)/shard_map/ppermute | solution.py:28
  101.3 13.1 %collective-permute-start.9 = (f32[7,128]{1,0:T(8,128)S(1)}, f32[7,128]{1,0:T(8,128)S(1)}, u32[]{:S(2)}, u32[]{:S(2)}) collective-permute-start(f32[7,128]{1,0:T(8,128)S(1)} %fusion.5), channel_id=1, source_target_pairs={{0,256},{1,257},{2,258},{3,259},{4,260},{5,261},{6,262},{7,263},{8... | collective-permute-start | bytes 10760 | tf_op jit(solution)/shard_map/ppermute | solution.py:28
  114.4 8.6 %collective-permute-start.10 = (f32[14,128]{1,0:T(8,128)S(1)}, f32[14,128]{1,0:T(8,128)S(1)}, u32[]{:S(2)}, u32[]{:S(2)}) collective-permute-start(f32[14,128]{1,0:T(8,128)S(1)} %pad_maximum_fusion.5), channel_id=1, source_target_pairs={{0,128},{1,129},{2,130},{3,131},{4,132},{5,133},{6,134},{7,135},{8... | collective-permute-start | bytes 21512 | tf_op jit(solution)/shard_map/ppermute | solution.py:28
  123.0 5.4 %collective-permute-start.11 = (f32[28,128]{1,0:T(8,128)S(1)}, f32[28,128]{1,0:T(8,128)S(1)}, u32[]{:S(2)}, u32[]{:S(2)}) collective-permute-start(f32[28,128]{1,0:T(8,128)S(1)} %pad_maximum_fusion.4), channel_id=1, source_target_pairs={{0,64},{1,65},{2,66},{3,67},{4,68},{5,69},{6,70},{7,71},{8,72},{9,... | collective-permute-start | bytes 43016 | tf_op jit(solution)/shard_map/ppermute | solution.py:28
  128.4 6.1 %collective-permute-start.12 = (f32[56,128]{1,0:T(8,128)S(1)}, f32[56,128]{1,0:T(8,128)S(1)}, u32[]{:S(2)}, u32[]{:S(2)}) collective-permute-start(f32[56,128]{1,0:T(8,128)S(1)} %pad_maximum_fusion.3), channel_id=1, source_target_pairs={{0,16},{1,17},{2,18},{3,19},{4,20},{5,21},{6,22},{7,23},{8,24},{9,... | collective-permute-start | bytes 86024 | tf_op jit(solution)/shard_map/ppermute | solution.py:28
  134.6 5.2 %collective-permute-start.13 = (f32[112,128]{1,0:T(8,128)S(1)}, f32[112,128]{1,0:T(8,128)S(1)}, u32[]{:S(2)}, u32[]{:S(2)}) collective-permute-start(f32[112,128]{1,0:T(8,128)S(1)} %pad_maximum_fusion.2), channel_id=1, source_target_pairs={{0,32},{1,33},{2,34},{3,35},{4,36},{5,37},{6,38},{7,39},{8,40},{9,... | collective-permute-start | bytes 172040 | tf_op jit(solution)/shard_map/ppermute | solution.py:28
  139.8 5.8 %collective-permute-start.14 = (f32[224,128]{1,0:T(8,128)S(1)}, f32[224,128]{1,0:T(8,128)S(1)}, u32[]{:S(2)}, u32[]{:S(2)}) collective-permute-start(f32[224,128]{1,0:T(8,128)S(1)} %pad_maximum_fusion.1), channel_id=1, source_target_pairs={{0,8},{1,9},{2,10},{3,11},{4,12},{5,13},{6,14},{7,15},{8,0},{9,1},... | collective-permute-start | bytes 344072 | tf_op jit(solution)/shard_map/ppermute | solution.py:28
  149.1 52.2 %copy-start.4 = (f32[64,384]{1,0:T(8,128)}, f32[64,384]{1,0:T(8,128)S(1)}, u32[]{:S(2)}) copy-start(f32[64,384]{1,0:T(8,128)S(1)} %get-tuple-element.70) | copy-start | bytes 294916
  149.1 52.1 %copy-start.5 = (f32[64,384]{1,0:T(8,128)}, f32[64,384]{1,0:T(8,128)S(1)}, u32[]{:S(2)}) copy-start(f32[64,384]{1,0:T(8,128)S(1)} %get-tuple-element.71) | copy-start | bytes 294916
  149.8 51.5 %copy-start.6 = (f32[48,512]{1,0:T(8,128)}, f32[48,512]{1,0:T(8,128)S(1)}, u32[]{:S(2)}) copy-start(f32[48,512]{1,0:T(8,128)S(1)} %get-tuple-element.68) | copy-start | bytes 294916
  149.8 51.6 %copy-start.7 = (f32[48,512]{1,0:T(8,128)}, f32[48,512]{1,0:T(8,128)S(1)}, u32[]{:S(2)}) copy-start(f32[48,512]{1,0:T(8,128)S(1)} %get-tuple-element.69) | copy-start | bytes 294916
  182.2 19.1 %copy-start.13 = (f32[4]{0:T(128)}, f32[4]{0:T(128)S(1)}, u32[]{:S(2)}) copy-start(f32[4]{0:T(128)S(1)} %get-tuple-element.123) | copy-start | bytes 52
